TPU v7x, 512 devices: a whole 4x4x16 slice. The times are simulated.
512 devices in a mesh: wide: 64 (over x, z), narrow: 8 (over y, core).
Axes of the slice: x: 4, y: 4, z: 16, core: 2. Of those that a mesh axis runs over, the one named last changes fastest.
Arguments:
- tokens: bfloat16 [49152, 2048], P('wide', 'narrow'), may hold values from -6 to 6
- norm_gain: float32 [2048], replicated, may hold values from 0.1 to 1.9
- qkv_weight: bfloat16 [2048, 3, 2048], P('wide', None, 'narrow'), may hold values from -0.125 to 0.125
- out_weight: bfloat16 [2048, 2048], P('wide', 'narrow'), may hold values from -0.25 to 0.25
- cache_pool: bfloat16 [1536, 128, 2, 2048], P('wide', None, None, 'narrow'), may hold values from -400 to 400, as said below
- prefix_pool: bfloat16 [2048, 2, 2048], P('wide', None, 'narrow'), may hold values from -6 to 6
- page_table: int32 [64, 24], P('wide'), may hold values from 0 to 23, each once within a row
- cache_len: int32 [64], P('wide'), may hold values from 512 to 3072
- group_ids: int32 [64], P('wide'), may hold values from 0 to 7, as said below
- group_pages: int32 [16], replicated, may hold values from 0 to 15, each once
Outputs:
- branch_out: bfloat16 [49152, 2048], P('wide', 'narrow')
- new_pages: bfloat16 [49152, 2, 2048], P('wide', None, 'narrow')
Inputs may be any that keep to these rules, and one draw needn't show every extreme that they name: `page_table`: each row is a permutation of the 24 pages of that request. `group_ids`: each group has 8 requests. `group_pages`: a permutation of the prefix pool's pages. `cache_pool`: keys are stored already rotated.
All inputs are finite; a program needn't handle non-finite values.
Results may differ from a plain program's by a relative error of at most 0.0095.
The roundings to bfloat16 on the way count: a program that leaves them out, or rounds other values in their place, can miss the bound.
Values may be sent and summed in bfloat16 or wider, within the bound.
No kernel may reach another device: no remote copies, remote signals or barrier semaphores. Data moves between devices by JAX's collectives and lax.ppermute only.
A program may use at most 128 MiB of HBM per device.

v0:
```python
import jax
import jax.numpy as jnp
from jax import lax
from jax.sharding import PartitionSpec as P

HEAD_DIM = 64
ROT = 16
PAGE = 128
KB = 4
PPAGES = 2
NEGATIVE = -1e30


def rotary(vectors, positions):
    half_rot = ROT // 2
    frequency = 10000.0 ** (-(jnp.arange(half_rot, dtype=jnp.float32) * 2.0 / ROT))
    angles = positions.astype(jnp.float32)[:, None] * frequency[None, :]
    cos_part = jnp.concatenate([jnp.cos(angles), jnp.cos(angles)], axis=1)[:, None, :]
    sine_part = jnp.concatenate([jnp.sin(angles), jnp.sin(angles)], axis=1)[:, None, :]
    rotated_in = vectors[..., :ROT]
    turned = jnp.concatenate([-rotated_in[..., half_rot:], rotated_in[..., :half_rot]], axis=-1)
    return jnp.concatenate(
        [rotated_in * cos_part + turned * sine_part, vectors[..., ROT:]], axis=-1
    )


def attend(running, queries, keys, values, key_valid):
    row_max, weight_sum, weighted = running
    scores = jnp.einsum("qhd,khd->hqk", queries, keys, preferred_element_type=jnp.float32) * 0.125
    scores = jnp.where(key_valid[None], scores, NEGATIVE)
    new_max = jnp.maximum(row_max, jnp.max(scores, axis=2))
    expo = jnp.where(key_valid[None], jnp.exp(scores - new_max[:, :, None]), 0.0)
    factor = jnp.exp(row_max - new_max)
    weight_sum = weight_sum * factor + jnp.sum(expo, axis=2)
    update = jnp.einsum(
        "hqk,khd->qhd", expo.astype(jnp.bfloat16), values, preferred_element_type=jnp.float32
    )
    weighted = weighted * jnp.transpose(factor)[:, :, None] + update
    return (new_max, weight_sum, weighted)


def local(
    tokens,
    norm_gain,
    qkv_weight,
    out_weight,
    cache_pool,
    prefix_pool,
    page_table,
    cache_len,
    group_ids,
    group_pages,
):
    span_rows = tokens.shape[0]
    local_width = qkv_weight.shape[2]
    heads_here = local_width // HEAD_DIM
    gathered = lax.all_gather(tokens, "narrow", axis=1, tiled=True)
    widened = gathered.astype(jnp.float32)
    row_mean = jnp.mean(widened, axis=1, keepdims=True)
    centered = widened - row_mean
    variance = jnp.mean(centered * centered, axis=1, keepdims=True)
    normed = (centered * lax.rsqrt(variance + 1e-05) * norm_gain).astype(jnp.bfloat16)
    piece_rows = lax.all_gather(qkv_weight, "wide", axis=0, tiled=True)
    piece_count = piece_rows.shape[0]
    columns = normed
    projected = jnp.dot(
        columns,
        piece_rows.reshape(piece_count, 3 * local_width),
        preferred_element_type=jnp.float32,
    )
    projected = projected.reshape(span_rows, 3, heads_here, HEAD_DIM)
    length = cache_len[0]
    offset = jnp.arange(span_rows, dtype=jnp.int32)
    positions = PPAGES * PAGE + length + offset
    queries = rotary(projected[:, 0], positions).astype(jnp.bfloat16)
    keys = rotary(projected[:, 1], positions).astype(jnp.bfloat16)
    values = projected[:, 2].astype(jnp.bfloat16)
    new_pages = jnp.stack(
        [keys.reshape(span_rows, local_width), values.reshape(span_rows, local_width)], axis=1
    )
    initial = (
        jnp.full((heads_here, span_rows), NEGATIVE, jnp.float32),
        jnp.zeros((heads_here, span_rows), jnp.float32),
        jnp.zeros((span_rows, heads_here, HEAD_DIM), jnp.float32),
    )
    running = attend(initial, queries, keys, values, offset[:, None] >= offset[None, :])
    my_group = group_ids[0]
    prefix_whole = lax.all_gather(prefix_pool, "wide", axis=0, tiled=True)
    prefix_pages = prefix_whole.reshape(-1, PAGE, 2, heads_here, HEAD_DIM)
    chosen = lax.dynamic_slice_in_dim(group_pages, my_group * PPAGES, PPAGES)
    key_rows = jnp.take(prefix_pages, chosen, axis=0).reshape(
        PPAGES * PAGE, 2, heads_here, HEAD_DIM
    )
    running = attend(
        running,
        queries,
        key_rows[:, 0],
        key_rows[:, 1],
        jnp.ones((span_rows, PPAGES * PAGE), dtype=bool),
    )
    page_list = page_table[0]
    block_keys = KB * PAGE
    blocks = (length + block_keys - 1) // block_keys
    key_offset = jnp.arange(block_keys, dtype=jnp.int32)

    def cache_block(block_index, state_now):
        page_ids = lax.dynamic_slice_in_dim(page_list, block_index * KB, KB)
        key_rows = jnp.take(cache_pool, page_ids, axis=0).reshape(
            block_keys, 2, heads_here, HEAD_DIM
        )
        key_valid = jnp.broadcast_to(
            (block_index * block_keys + key_offset < length)[None, :], (span_rows, block_keys)
        )
        return attend(state_now, queries, key_rows[:, 0], key_rows[:, 1], key_valid)

    running = lax.fori_loop(0, blocks, cache_block, running)
    head_values = (
        (running[2] / jnp.transpose(running[1])[:, :, None])
        .astype(jnp.bfloat16)
        .reshape(span_rows, local_width)
    )
    all_heads = lax.all_gather(head_values, "narrow", axis=1, tiled=True)
    columns = all_heads
    branch_out = jnp.dot(
        columns,
        lax.all_gather(out_weight, "wide", axis=0, tiled=True),
        preferred_element_type=jnp.float32,
    )
    return (branch_out.astype(jnp.bfloat16), new_pages)


def solution(mesh):
    placed = (
        P("wide", "narrow"),
        P(),
        P("wide", None, "narrow"),
        P("wide", "narrow"),
        P("wide", None, None, "narrow"),
        P("wide", None, "narrow"),
        P("wide", None),
        P("wide"),
        P("wide"),
        P(),
    )
    return jax.shard_map(
        local,
        mesh=mesh,
        in_specs=placed,
        out_specs=(P("wide", "narrow"), P("wide", None, "narrow")),
        check_vma=False,
    )
```

profile of v0, /device:TPU:1, one launch (start us, length us, event | category | flops | bytes accessed | tf_op | source)
XLA Modules:
  0.0 524.0 jit_solution(7641525677525579463)
XLA Ops:
  7.2 0.0 all-gather.10.cloned.1.call-start
  7.2 0.7 all-gather.10.cloned.1.call-update
  7.9 0.0 all-gather.6.cloned.1.call-start
  7.9 0.7 all-gather.6.cloned.1.call-update
  8.6 0.0 all-gather.8.cloned.1.call-start
  8.7 0.7 all-gather.8.cloned.1.call-update
  9.4 0.0 all-gather.14.cloned.1.call-start
  9.4 0.5 all-gather.14.cloned.1.call-update
  10.0 0.0 all-gather.12.cloned.1.call-start
  10.7 1.0 iota_compare_fusion
  12.3 0.7 compare_and_fusion.1
  13.1 0.1 broadcast_bitcast_fusion.1
  13.2 0.2 multiply_cosine_fusion
  13.4 134.0 %all-gather.10.cloned.1.call-done = bf16[2048,2,256]{2,1,0:T(2,128)(2,1)} async-done(((bf16[32,2,256]{2,1,0:T(2,128)(2,1)}), bf16[2048,2,256]{2,1,0:T(2,128)(2,1)}) %all-gather.10.cloned.1.call-update) | async-done | bytes 2097168 | tf_op jit(solution)/shard_map/all_gather | solution.py:88
  147.3 8.8 %reshape.131 = bf16[16,128,2,4,64]{4,3,2,1,0:T(4,128)(2,1)} reshape(bf16[2048,2,256]{2,1,0:T(2,128)(2,1)} %all-gather.10.cloned.1.call-done) | data formatting | bytes 4194304 | tf_op jit(solution)/shard_map/reshape | solution.py:89
  156.2 5.8 %copy.32 = bf16[16,128,2,4,64]{1,4,3,2,0:T(8,128)(2,1)S(1)} copy(bf16[16,128,2,4,64]{4,3,2,1,0:T(4,128)(2,1)} %reshape.131) | data formatting | bytes 4194304 | tf_op jit(solution)/shard_map/reshape | solution.py:89
  161.9 0.6 gather_fusion.1
  162.6 0.0 copy-start.4
  162.6 31.8 %all-gather.6.cloned.1.call-done = bf16[768,2048]{1,0:T(8,128)(2,1)} async-done(((bf16[768,256]{1,0:T(8,128)(2,1)}), bf16[768,2048]{1,0:T(8,128)(2,1)}) %all-gather.6.cloned.1.call-update) | async-done | bytes 3145744 | tf_op jit(solution)/shard_map/all_gather | solution.py:57
  194.4 2.5 convert_reduce_fusion
  197.0 2.8 fusion.27
  199.8 132.6 %all-gather.8.cloned.1.call-done = bf16[2048,3,256]{2,0,1:T(8,128)(2,1)} async-done(((bf16[32,3,256]{2,0,1:T(8,128)(2,1)}), bf16[2048,3,256]{2,0,1:T(8,128)(2,1)}) %all-gather.8.cloned.1.call-update) | async-done | bytes 3145744 | tf_op jit(solution)/shard_map/all_gather | solution.py:63
  332.4 4.7 copy.30
  337.1 0.0 copy-done.4
  337.1 4.6 fusion.34
  341.8 0.0 copy-start.1
  341.8 0.1 slice_bitcast_fusion.4
  342.1 0.6 multiply_reduce_fusion
  342.8 0.5 copy-done.1
  343.3 1.8 fusion.22
  345.1 2.3 fusion.26
  347.4 2.8 fusion.57
  350.2 0.5 fusion.40
  350.8 0.7 fusion.51
  351.5 21.3 %while.15 = (s32[]{:T(128)}, f32[4,768]{1,0:T(4,128)S(1)}, f32[4,768]{1,0:T(4,128)S(1)}, f32[768,4,64]{0,2,1:T(8,128)S(1)}, s32[]{:T(128)}, /*index=5*/s32[]{:T(...) while((s32[]{:T(128)}, f32[4,768]{1,0:T(4,128)S(1)}, ...), condition=%wide.region_9.10_spmd.clone, body=%wide.region_6.9_spmd.clone.sunk | while | flops 423767072 | bytes 25763612 | solution.py:116
  351.5 0.7 fusion.88
  352.2 0.1 compare_and_fusion.3
  352.3 0.1 broadcast_bitcast_fusion.3
  352.4 3.5 gather_fusion
  355.9 0.8 copy.47
  356.7 0.2 gather.23
  356.9 0.1 broadcast_select_fusion.2
  357.0 1.4 bitcast_reduce_fusion.2
  358.4 2.0 fusion.90
  360.3 1.7 fusion.91
  362.1 0.7 fusion.88
  362.7 0.1 compare_and_fusion.3
  362.8 0.1 broadcast_bitcast_fusion.3
  362.9 3.5 gather_fusion
  366.4 0.8 copy.47
  367.2 0.2 gather.23
  367.4 0.1 broadcast_select_fusion.2
  367.5 1.4 bitcast_reduce_fusion.2
  368.9 2.0 fusion.90
  370.9 1.7 fusion.91
  372.8 0.8 divide_convert_fusion
  373.6 0.0 all-gather.12.cloned.1.call-update
  373.6 1.2 slice.106
  374.8 0.6 copy.37
  375.5 0.6 copy.36
  376.1 2.7 pad_maximum_fusion
  378.8 90.2 %all-gather.14.cloned.1.call-done = bf16[2048,256]{1,0:T(8,128)(2,1)} async-done(((bf16[32,256]{1,0:T(8,128)(2,1)}), bf16[2048,256]{1,0:T(8,128)(2,1)}) %all-gather.14.cloned.1.call-update) | async-done | bytes 1048592 | tf_op jit(solution)/shard_map/all_gather | solution.py:126
  469.0 44.6 %all-gather.12.cloned.1.call-done = bf16[768,2048]{0,1:T(8,128)(2,1)} async-done(((bf16[768,256]{0,1:T(8,128)(2,1)}), bf16[768,2048]{0,1:T(8,128)(2,1)}) %all-gather.12.cloned.1.call-update) | async-done | bytes 3145744 | tf_op jit(solution)/shard_map/all_gather | solution.py:122
  513.6 3.9 convolution_convert_fusion
  (31 shorter events, 0.5 us)
Async XLA Ops:
  7.2 140.2 %all-gather.10.cloned.1.call-start = ((), (), s32[]{:S(2)}) async-start(), calls=%async_computation.2 | async-start | bytes 2129920 | tf_op jit(solution)/shard_map/all_gather | solution.py:88
  7.9 186.5 %all-gather.6.cloned.1.call-start = ((), (), s32[]{:S(2)}) async-start(), calls=%async_computation | async-start | bytes 3538944 | tf_op jit(solution)/shard_map/all_gather | solution.py:57
  8.6 323.8 %all-gather.8.cloned.1.call-start = ((), (), s32[]{:S(2)}) async-start(), calls=%async_computation.1 | async-start | bytes 3194880 | tf_op jit(solution)/shard_map/all_gather | solution.py:63
  9.4 459.6 %all-gather.14.cloned.1.call-start = ((), (), s32[]{:S(2)}) async-start(), calls=%async_computation.4 | async-start | bytes 1064960 | tf_op jit(solution)/shard_map/all_gather | solution.py:126
  10.0 503.6 %all-gather.12.cloned.1.call-start = ((), (), s32[]{:S(2)}) async-start(), calls=%async_computation.3 | async-start | bytes 3538944 | tf_op jit(solution)/shard_map/all_gather | solution.py:122
  162.6 174.6 %copy-start.4 = (f32[2048]{0:T(1024)S(1)}, f32[2048]{0:T(1024)}, u32[]{:S(2)}) copy-start(f32[2048]{0:T(1024)} %param.13) | copy-start | bytes 24580
  194.4 142.7 %copy-start = (bf16[768,2048]{1,0:T(8,128)(2,1)S(1)}, bf16[768,2048]{1,0:T(8,128)(2,1)}, u32[]{:S(2)}) copy-start(bf16[768,2048]{1,0:T(8,128)(2,1)} %all-gather.6.cloned.1.call-done) | copy-start | bytes 9437188
  341.8 5.7 %copy-start.2 = (f32[768,3,4,64]{0,3,2,1:T(8,128)}, f32[768,3,4,64]{0,3,2,1:T(8,128)S(1)}, u32[]{:S(2)}) copy-start(f32[768,3,4,64]{0,3,2,1:T(8,128)S(1)} %fusion.34) | copy-start | bytes 7077892
  341.8 1.5 copy-start.1
  350.2 1.3 copy-start.3
Sparse Core Ops, SparseCore 0:
  10.9 136.3 all-gather.9
  149.5 44.9 all-gather.5
  197.4 134.9 all-gather.7
  335.2 133.7 all-gather.13
  471.5 42.0 all-gather.11
where the time goes:
time: 525 us; the launch traced here: 524 us
  waiting for transfers between devices  436 us (83%)
  local copies, waits for them, and re-layouts  32.3 us (6%)
  matrix products  20.6 us (4%)
  other arithmetic  19.5 us (4%)
  between operations  15.3 us (3%)
    all_gather x1, waiting for transfers between devices, local(): prefix_whole = lax.all_gather(prefix_pool, 'wide', axis=0, tiled=True)  134 us
    all_gather x1, waiting for transfers between devices, local(): piece_rows = lax.all_gather(qkv_weight, 'wide', axis=0, tiled=True)  133 us
    all_gather x1, waiting for transfers between devices, local(): lax.all_gather(out_weight, 'wide', axis=0, tiled=True)  90.2 us
    all_gather x1, waiting for transfers between devices, local(): all_heads = lax.all_gather(head_values, 'narrow', axis=1, tiled=True)  44.6 us
    all_gather x1, waiting for transfers between devices, local(): gathered = lax.all_gather(tokens, 'narrow', axis=1, tiled=True)  31.8 us
    reshape x2, local copies, waits for them, and re-layouts, local(): prefix_pages = prefix_whole.reshape(-1, PAGE, 2, heads_here, HEAD_DIM)  14.6 us
  transfers between devices with their start and end apart: 5, of which 5 were waited for; matrix products, arithmetic and copies ran while one was open for 13% of the time, Pallas kernels for 0%

commit v1 on v0

--- a/solution.py
+++ b/solution.py
@@ -1,3 +1,4 @@
+import functools
 import jax
 import jax.numpy as jnp
 from jax import lax
@@ -9,6 +10,18 @@
 KB = 4
 PPAGES = 2
 NEGATIVE = -1e30
+
+
+def produce_tokens(inp, row_dim):
+    return jnp.concatenate(
+        lax.all_to_all(
+            jnp.stack([inp for _ in range(lax.axis_size("wide"))], axis=0), "wide", 0, 0
+        ),
+        row_dim,
+    )
+
+
+check_steps_all_up = functools.partial(produce_tokens, row_dim=0)
 
 
 def rotary(vectors, positions):
@@ -122,9 +135,7 @@
     all_heads = lax.all_gather(head_values, "narrow", axis=1, tiled=True)
     columns = all_heads
     branch_out = jnp.dot(
-        columns,
-        lax.all_gather(out_weight, "wide", axis=0, tiled=True),
-        preferred_element_type=jnp.float32,
+        columns, check_steps_all_up(out_weight), preferred_element_type=jnp.float32
     )
     return (branch_out.astype(jnp.bfloat16), new_pages)
 

time: 525 us -> 488 us (0.930)
  the two profiles are of different devices: /device:TPU:1 before, /device:TPU:38 now
where the time goes in v1:
time: 488 us; the launch traced here: 487 us
  waiting for transfers between devices  346 us (71%)
  starting transfers between devices  52.2 us (11%)
  local copies, waits for them, and re-layouts  33.5 us (7%)
  matrix products  20.6 us (4%)
  other arithmetic  19.5 us (4%)
  between operations  15.3 us (3%)
    all_gather x1, waiting for transfers between devices, local(): prefix_whole = lax.all_gather(prefix_pool, 'wide', axis=0, tiled=True)  142 us
    all_gather x1, waiting for transfers between devices, local(): piece_rows = lax.all_gather(qkv_weight, 'wide', axis=0, tiled=True)  140 us
    all_to_all x1, starting transfers between devices, produce_tokens(): lax.all_to_all(jnp.stack([inp for _ in range(lax.axis_size('wide'))], axi...  52 us
    all_to_all x1, waiting for transfers between devices, produce_tokens(): lax.all_to_all(jnp.stack([inp for _ in range(lax.axis_size('wide'))], axi...  38.7 us
    all_gather x1, waiting for transfers between devices, local(): gathered = lax.all_gather(tokens, 'narrow', axis=1, tiled=True)  23 us
    reshape x2, local copies, waits for them, and re-layouts, local(): prefix_pages = prefix_whole.reshape(-1, PAGE, 2, heads_here, HEAD_DIM)  14.6 us
  transfers between devices with their start and end apart: 5, of which 4 were waited for; matrix products, arithmetic and copies ran while one was open for 6% of the time, Pallas kernels for 0%

profile of v1, /device:TPU:38, one launch (start us, length us, event | category | flops | bytes accessed | tf_op | source)
XLA Modules:
  0.0 487.3 jit_solution(10673735141496898816)
XLA Ops:
  7.2 0.0 all-gather.9.cloned.1.call-start
  7.2 0.7 all-gather.9.cloned.1.call-update
  7.9 0.0 all-gather.5.cloned.1.call-start
  7.9 0.7 all-gather.5.cloned.1.call-update
  8.6 0.0 all-gather.7.cloned.1.call-start
  8.7 0.7 all-gather.7.cloned.1.call-update
  9.4 0.0 all-gather.11.cloned.1.call-start
  10.8 0.7 compare_and_fusion.1
  11.5 0.2 multiply_cosine_fusion
  11.7 1.0 iota_compare_fusion
  12.7 0.1 broadcast_bitcast_fusion.1
  12.8 141.8 %all-gather.9.cloned.1.call-done = bf16[2048,2,256]{2,1,0:T(2,128)(2,1)} async-done(((bf16[32,2,256]{2,1,0:T(2,128)(2,1)}), bf16[2048,2,256]{2,1,0:T(2,128)(2,1)}) %all-gather.9.cloned.1.call-update) | async-done | bytes 2097168 | tf_op jit(solution)/shard_map/all_gather | solution.py:101
  154.6 8.8 %reshape.137 = bf16[16,128,2,4,64]{4,3,2,1,0:T(4,128)(2,1)} reshape(bf16[2048,2,256]{2,1,0:T(2,128)(2,1)} %all-gather.9.cloned.1.call-done) | data formatting | bytes 4194304 | tf_op jit(solution)/shard_map/reshape | solution.py:102
  163.4 5.8 %copy.32 = bf16[16,128,2,4,64]{1,4,3,2,0:T(8,128)(2,1)S(1)} copy(bf16[16,128,2,4,64]{4,3,2,1,0:T(4,128)(2,1)} %reshape.137) | data formatting | bytes 4194304 | tf_op jit(solution)/shard_map/reshape | solution.py:102
  169.2 0.6 gather_fusion.1
  169.8 0.0 copy-start.5
  169.8 23.0 %all-gather.5.cloned.1.call-done = bf16[768,2048]{1,0:T(8,128)(2,1)} async-done(((bf16[768,256]{1,0:T(8,128)(2,1)}), bf16[768,2048]{1,0:T(8,128)(2,1)}) %all-gather.5.cloned.1.call-update) | async-done | bytes 3145744 | tf_op jit(solution)/shard_map/all_gather | solution.py:70
  192.8 2.5 convert_reduce_fusion
  195.3 2.8 fusion.27
  198.2 140.4 %all-gather.7.cloned.1.call-done = bf16[2048,3,256]{2,0,1:T(8,128)(2,1)} async-done(((bf16[32,3,256]{2,0,1:T(8,128)(2,1)}), bf16[2048,3,256]{2,0,1:T(8,128)(2,1)}) %all-gather.7.cloned.1.call-update) | async-done | bytes 3145744 | tf_op jit(solution)/shard_map/all_gather | solution.py:76
  338.5 4.7 copy.30
  343.3 4.6 fusion.34
  347.9 0.0 copy-start.1
  347.9 0.1 slice_bitcast_fusion.4
  348.2 0.6 multiply_reduce_fusion
  348.9 0.5 copy-done.1
  349.4 1.8 fusion.22
  351.3 2.3 fusion.26
  353.6 0.0 copy-done.2
  353.6 2.8 fusion.57
  356.4 0.5 fusion.40
  356.9 0.7 fusion.51
  357.6 0.0 copy-start.3
  357.7 21.3 %while.15 = (s32[]{:T(128)}, f32[4,768]{1,0:T(4,128)S(1)}, f32[4,768]{1,0:T(4,128)S(1)}, f32[768,4,64]{0,2,1:T(8,128)S(1)}, s32[]{:T(128)}, /*index=5*/s32[]{:T(...) while((s32[]{:T(128)}, f32[4,768]{1,0:T(4,128)S(1)}, ...), condition=%wide.region_9.10_spmd.clone, body=%wide.region_6.9_spmd.clone.sunk | while | flops 423767072 | bytes 25763612 | solution.py:129
  357.7 0.7 fusion.88
  358.3 0.1 compare_and_fusion.3
  358.4 0.1 broadcast_bitcast_fusion.3
  358.5 3.5 gather_fusion
  362.0 0.8 copy.47
  362.9 0.2 gather.23
  363.1 0.1 broadcast_select_fusion.2
  363.1 1.4 bitcast_reduce_fusion.2
  364.5 2.0 fusion.90
  366.5 1.7 fusion.91
  368.2 0.7 fusion.88
  368.9 0.1 compare_and_fusion.3
  369.0 0.1 broadcast_bitcast_fusion.3
  369.0 3.5 gather_fusion
  372.5 0.8 copy.47
  373.4 0.2 gather.23
  373.6 0.1 broadcast_select_fusion.2
  373.6 1.4 bitcast_reduce_fusion.2
  375.0 2.0 fusion.90
  377.0 1.7 fusion.91
  379.0 0.8 divide_convert_fusion
  379.8 0.0 all-gather.11.cloned.1.call-update
  379.8 1.1 stack.4
  380.9 52.0 %all-to-all-start = ((bf16[64,32,256]{2,1,0:T(8,128)(2,1)}), bf16[64,32,256]{2,1,0:T(8,128)(2,1)}, u32[]{:S(2)}, u32[]{:S(2)}) async-start(bf16[64,32,256]{2,1,0:T(8,128)(2,1)} %stack.4), calls=%async_computation | async-start | bytes 2097152 | tf_op jit(solution)/shard_map/all_to_all | solution.py:17
  432.9 1.2 slice.106
  434.1 0.6 copy.37
  434.8 0.6 copy.36
  435.4 2.7 pad_maximum_fusion
  438.1 38.7 %all-to-all-done = bf16[64,32,256]{2,1,0:T(8,128)(2,1)} async-done(((bf16[64,32,256]{2,1,0:T(8,128)(2,1)}), bf16[64,32,256]{2,1,0:T(8,128)(2,1)}, u32[]{:S(2)}, u32[]{:S(2)}) %all-to-all-start) | async-done | bytes 1048608 | tf_op jit(solution)/shard_map/all_to_all | solution.py:17
  476.8 3.9 convolution_convert_fusion
  (33 shorter events, 0.5 us)
Async XLA Ops:
  7.2 147.4 %all-gather.9.cloned.1.call-start = ((), (), s32[]{:S(2)}) async-start(), calls=%async_computation.3 | async-start | bytes 2129920 | tf_op jit(solution)/shard_map/all_gather | solution.py:101
  7.9 184.9 %all-gather.5.cloned.1.call-start = ((), (), s32[]{:S(2)}) async-start(), calls=%async_computation.1 | async-start | bytes 3538944 | tf_op jit(solution)/shard_map/all_gather | solution.py:70
  8.6 329.9 %all-gather.7.cloned.1.call-start = ((), (), s32[]{:S(2)}) async-start(), calls=%async_computation.2 | async-start | bytes 3194880 | tf_op jit(solution)/shard_map/all_gather | solution.py:76
  9.4 467.4 %all-gather.11.cloned.1.call-start = ((), (), s32[]{:S(2)}) async-start(), calls=%async_computation.4 | async-start | bytes 3538944 | tf_op jit(solution)/shard_map/all_gather | solution.py:135
  169.8 173.5 %copy-start.5 = (f32[2048]{0:T(1024)S(1)}, f32[2048]{0:T(1024)}, u32[]{:S(2)}) copy-start(f32[2048]{0:T(1024)} %param.13) | copy-start | bytes 24580
  192.8 150.5 %copy-start = (bf16[768,2048]{1,0:T(8,128)(2,1)S(1)}, bf16[768,2048]{1,0:T(8,128)(2,1)}, u32[]{:S(2)}) copy-start(bf16[768,2048]{1,0:T(8,128)(2,1)} %all-gather.5.cloned.1.call-done) | copy-start | bytes 9437188
  347.9 5.7 %copy-start.2 = (f32[768,3,4,64]{0,3,2,1:T(8,128)}, f32[768,3,4,64]{0,3,2,1:T(8,128)S(1)}, u32[]{:S(2)}) copy-start(f32[768,3,4,64]{0,3,2,1:T(8,128)S(1)} %fusion.34) | copy-start | bytes 7077892
  347.9 1.5 copy-start.1
  356.4 1.3 copy-start.4
  357.6 22.1 %copy-start.3 = (bf16[32,256]{1,0:T(8,128)(2,1)S(1)}, bf16[32,256]{1,0:T(8,128)(2,1)}, u32[]{:S(2)}) copy-start(bf16[32,256]{1,0:T(8,128)(2,1)} %param.15) | copy-start | bytes 49156
  380.9 95.9 %all-to-all-start = ((bf16[64,32,256]{2,1,0:T(8,128)(2,1)}), bf16[64,32,256]{2,1,0:T(8,128)(2,1)}, u32[]{:S(2)}, u32[]{:S(2)}) async-start(bf16[64,32,256]{2,1,0:T(8,128)(2,1)} %stack.4), calls=%async_computation | async-start | bytes 2097152 | tf_op jit(solution)/shard_map/all_to_all | solution.py:17
Sparse Core Ops, SparseCore 0:
  10.9 143.6 all-gather.8
  156.7 36.0 all-gather.4
  195.7 142.7 all-gather.6
  379.9 72.7 all-gather.10
